TPU v7x, 128 devices: a whole 4x4x4 slice. The times are simulated.
128 devices in a mesh: dom: 16 (over x, z_hi, core), cls: 8 (over z_lo, y).
Axes of the slice: x: 4, y: 4, z: 4 (z_hi: 2, z_lo: 2; z = z_hi * 2 + z_lo), core: 2. Of those that a mesh axis runs over, the one named last changes fastest.
Arguments:
- particles: bfloat16 [2048, 16384], P(('dom', 'cls')), may hold values from -6 to 6
- averages: float32 [256, 16384], P('cls'), may hold values from -4 to 4
- prior_mass: float32 [256], P('cls'), may hold values from 1 to 8
- group_ids: int32 [4, 2048, 1], P(None, ('dom', 'cls')), may hold values from 0 to 7; in each aligned block of 16 rows (0 to 15, 16 to 31, ..., all dimensions but the last counted through in order) at most 6 rows name the same one
- class_ids: int32 [4, 2048], P(None, ('dom', 'cls')), may hold values from 0 to 31
- rot_ids: int32 [4, 2048], P(None, ('dom', 'cls')), may hold values from 0 to 63
- weights: bfloat16 [4, 2048], P(None, ('dom', 'cls')), may hold values from 0.25 to 4
- owners: int32 [4], replicated, may hold values from 0 to 7
Outputs:
- scores: float32 [4, 2048, 2048], P(None, ('dom', 'cls'))
- final_averages: float32 [256, 16384], P('cls')
Inputs may be any that keep to these rules, and one draw needn't show every extreme that they name: `group_ids`: in every step, at most 6 of the 16 particles of one device name one class group; in every step some device's particles reach 6 for some group.
All inputs are finite; a program needn't handle non-finite values.
Results may differ from a plain program's by a relative error of at most 0.0027.
Values may be sent and summed in bfloat16 or wider, within the bound.
No kernel may reach another device: no remote copies, remote signals or barrier semaphores. Data moves between devices by JAX's collectives and lax.ppermute only.
A program may use at most 256 MiB of HBM per device.

v0:
```python
import math
import jax
import jax.numpy as jnp
from jax import lax
from jax.sharding import PartitionSpec as P

RADII = 128
ANGLES = 128
ROT = 64
STEPS = 4
ASTEP = 2


def from_root(block, axis, owner):
    block = jnp.where(lax.axis_index(axis) == owner, block, jnp.zeros_like(block))
    return lax.psum(block, axis)


def rotate_each(images, shifts, angles):
    angle_idx = jnp.arange(angles, dtype=jnp.int32)
    index = (angle_idx[None, :] - shifts[:, None]) % angles
    return jnp.take_along_axis(images, index[:, None, :], axis=2)


def per_device(particles, averages, prior_mass, group_ids, class_ids, rot_ids, weights, owners):
    per_dev = particles.shape[0]
    pixels = particles.shape[1]
    groups = lax.axis_size("cls")
    per_group = averages.shape[0]
    capacity = per_dev * 3 // 8
    slots = groups * capacity
    cube = particles.reshape(per_dev, RADII, ANGLES)
    doubled = jnp.concatenate([cube, cube], axis=2)
    scale = 1.0 / math.sqrt(pixels)
    turns_block = min(ROT, max(8, 512 // per_dev))
    block_starts = list(range(0, ROT, turns_block))
    current = averages
    all_scores = []
    for step in range(STEPS):
        shifts = rot_ids[step] * ASTEP
        rotated = rotate_each(cube, shifts, ANGLES).reshape(per_dev, pixels)
        target = group_ids[step, :, 0]
        onehot_group = (target[:, None] == jnp.arange(groups, dtype=jnp.int32)[None, :]).astype(
            jnp.int32
        )
        rank = jnp.sum((jnp.cumsum(onehot_group, axis=0) - 1) * onehot_group, axis=1)
        slot_of = target * capacity + rank
        placing = (slot_of[None, :] == jnp.arange(slots, dtype=jnp.int32)[:, None]).astype(
            jnp.bfloat16
        )
        send_images = jnp.dot(placing, rotated, preferred_element_type=jnp.float32).astype(
            jnp.bfloat16
        )
        class_hot = (
            class_ids[step][:, None] == jnp.arange(per_group, dtype=jnp.int32)[None, :]
        ).astype(jnp.bfloat16)
        weighted_hot = class_hot * weights[step][:, None]
        send_weights = jnp.dot(placing, weighted_hot, preferred_element_type=jnp.float32).astype(
            jnp.bfloat16
        )
        got_images, got_weights = (
            lax.all_to_all(send_images, "cls", split_axis=0, concat_axis=0, tiled=True),
            lax.all_to_all(send_weights, "cls", split_axis=0, concat_axis=0, tiled=True),
        )
        partial_value = lax.dot_general(
            got_weights, got_images, (((0,), (0,)), ((), ())), preferred_element_type=jnp.float32
        )
        counts = jnp.sum(got_weights.astype(jnp.float32), axis=0)
        totals, mass = lax.psum((partial_value, counts), "dom")
        current = (prior_mass[:, None] * current + totals) / (prior_mass + mass)[:, None]
        refs = from_root(current.astype(jnp.bfloat16), "cls", owners[step])
        pieces = []
        for first in block_starts:
            count = min(turns_block, ROT - first)
            views = [
                doubled[:, :, ANGLES - turn * ASTEP : 2 * ANGLES - turn * ASTEP]
                for turn in range(first, first + count)
            ]
            rolled = jnp.stack(views, axis=1).reshape(per_dev * count, pixels)
            product = lax.dot_general(
                rolled, refs, (((1,), (1,)), ((), ())), preferred_element_type=jnp.float32
            )
            pieces.append(product.reshape(per_dev, count * per_group))
        stacked = jnp.concatenate(pieces, axis=1)
        all_scores.append(stacked * scale)
    return (jnp.stack(all_scores, axis=0), current)


def solution(mesh):
    return jax.shard_map(
        per_device,
        mesh=mesh,
        in_specs=(
            P(("dom", "cls"), None),
            P("cls", None),
            P("cls"),
            P(None, ("dom", "cls"), None),
            P(None, ("dom", "cls")),
            P(None, ("dom", "cls")),
            P(None, ("dom", "cls")),
            P(),
        ),
        out_specs=(P(None, ("dom", "cls"), None), P("cls", None)),
        check_vma=False,
    )
```

profile of v0, /device:TPU:1, one launch (start us, length us, event | category | flops | bytes accessed | tf_op | source)
XLA Modules:
  0.0 682.3 jit_solution(3866032299633491612)
XLA Ops:
  12.0 6.4 all-to-all-start.6
  20.8 11.1 %gather_fusion.3 = bf16[2048,128]{1,0:T(8,128)(2,1)S(1)} fusion(bf16[16,128,128]{1,2,0:T(8,128)(2,1)S(1)} %copy.50, s32[2048]{0:T(1024)S(1)} %get-tuple-element.115), kind=kCustom, calls=%fused_computation.3.clone | custom fusion | bytes 1064960 | tf_op jit(solution)/shard_map/jit(take_along_axis)/gather | solution.py:22
  34.1 5.1 all-to-all-start.4
  65.3 11.1 %gather_fusion.2 = bf16[2048,128]{1,0:T(8,128)(2,1)S(1)} fusion(bf16[16,128,128]{1,2,0:T(8,128)(2,1)S(1)} %copy.50, s32[2048]{0:T(1024)S(1)} %get-tuple-element.116), kind=kCustom, calls=%fused_computation.2.clone | custom fusion | bytes 1064960 | tf_op jit(solution)/shard_map/jit(take_along_axis)/gather | solution.py:22
  79.0 13.3 %all-to-all-done.7 = bf16[8,6,16384]{2,1,0:T(8,128)(2,1)} async-done(((bf16[8,6,16384]{2,1,0:T(8,128)(2,1)}), bf16[8,6,16384]{2,1,0:T(8,128)(2,1)}, u32[]{:S(2)}, u32[]{:S(2)}) %all-to-all-start.7) | async-done | bytes 1572896 | tf_op jit(solution)/shard_map/all_to_all | solution.py:62
  96.8 11.1 %gather_fusion.1 = bf16[2048,128]{1,0:T(8,128)(2,1)S(1)} fusion(bf16[16,128,128]{1,2,0:T(8,128)(2,1)S(1)} %copy.50, s32[2048]{0:T(1024)S(1)} %get-tuple-element.117), kind=kCustom, calls=%fused_computation.1.clone | custom fusion | bytes 1064960 | tf_op jit(solution)/shard_map/jit(take_along_axis)/gather | solution.py:22
  110.6 13.2 %all-to-all-done.5 = bf16[8,6,16384]{2,1,0:T(8,128)(2,1)} async-done(((bf16[8,6,16384]{2,1,0:T(8,128)(2,1)}), bf16[8,6,16384]{2,1,0:T(8,128)(2,1)}, u32[]{:S(2)}, u32[]{:S(2)}) %all-to-all-start.5) | async-done | bytes 1572896 | tf_op jit(solution)/shard_map/all_to_all | solution.py:62
  128.2 11.1 %gather_fusion = bf16[2048,128]{1,0:T(8,128)(2,1)S(1)} fusion(bf16[16,128,128]{1,2,0:T(8,128)(2,1)S(1)} %copy.50, s32[2048]{0:T(1024)S(1)} %get-tuple-element.118), kind=kCustom, calls=%fused_computation.clone | custom fusion | bytes 1064960 | tf_op jit(solution)/shard_map/jit(take_along_axis)/gather | solution.py:22
  141.9 13.3 %all-to-all-done.3 = bf16[8,6,16384]{2,1,0:T(8,128)(2,1)} async-done(((bf16[8,6,16384]{2,1,0:T(8,128)(2,1)}), bf16[8,6,16384]{2,1,0:T(8,128)(2,1)}, u32[]{:S(2)}, u32[]{:S(2)}) %all-to-all-start.3) | async-done | bytes 1572896 | tf_op jit(solution)/shard_map/all_to_all | solution.py:62
  171.6 15.1 %all-to-all-done.1 = bf16[8,6,16384]{2,1,0:T(8,128)(2,1)} async-done(((bf16[8,6,16384]{2,1,0:T(8,128)(2,1)}), bf16[8,6,16384]{2,1,0:T(8,128)(2,1)}, u32[]{:S(2)}, u32[]{:S(2)}) %all-to-all-start.1) | async-done | bytes 1572896 | tf_op jit(solution)/shard_map/all_to_all | solution.py:62
  216.0 34.7 %all-reduce = (f32[32]{0:T(128)S(1)}, f32[32]{0:T(128)S(1)}, f32[32]{0:T(128)S(1)}, f32[32]{0:T(128)S(1)}) all-reduce(f32[32]{0:T(128)S(1)} %convert_reduce_fusion, f32[32]{0:T(128)S(1)} %convert_reduce_fusion.1, f32[32]{0:T(128)S(1)} %convert_reduce_fusion.2, f32[32]{0:T(128)S(1)} %convert_reduce_fusion.3), channel_id=1, replica_groups=mesh['dom'=16,'cls'=8] {'dom'}, use_global_device_ids=true, to_apply=%region_22.24 | all-reduce | flops 128 | bytes 1024 | tf_op jit(solution)/shard_map/psum | solution.py:69
  250.7 146.9 %all-reduce.6.cloned.1.call-done = (f32[32,16384]{1,0:T(8,128)}, f32[32,16384]{1,0:T(8,128)}, f32[32,16384]{1,0:T(8,128)}, f32[32,16384]{1,0:T(8,128)}) async-done(((f32[32,16384]{1,0:T(8,128)}, f32[32,16384]{1,0:T(8,128)}, f32[32,16384]{1,0:T(8,128)}, f32[32,16384]{1,0:T(8,128)}), (f32[32,16384]{1,0:T(8,128)}, f32[32,16384]{1,0:T(8,128)}, f32[32,16384]{1,0:T(8,128)}, ...) | async-done | bytes 8388624 | tf_op jit(solution)/shard_map/psum | solution.py:69
  401.8 4.9 convert_select_fusion
  428.6 14.3 %copy.48 = bf16[16,32,128,128]{3,2,1,0:T(8,128)(2,1)} copy(bf16[16,32,128,128]{3,2,0,1:T(8,128)(2,1)} %get-tuple-element.21) | data formatting | bytes 33554432 | tf_op jit(solution)/shard_map/stack | solution.py:79
  442.9 14.2 %copy.55 = bf16[16,32,128,128]{3,2,1,0:T(8,128)(2,1)} copy(bf16[16,32,128,128]{3,2,0,1:T(8,128)(2,1)} %get-tuple-element.22) | data formatting | bytes 33554432 | tf_op jit(solution)/shard_map/stack | solution.py:79
  457.1 53.9 %all-reduce.8.cloned.1.call-done = (bf16[32,16384]{1,0:T(8,128)(2,1)}, bf16[32,16384]{1,0:T(8,128)(2,1)}, bf16[32,16384]{1,0:T(8,128)(2,1)}, bf16[32,16384]{1,0:T(8,128)(2,1)}) async-done(((bf16[32,16384]{1,0:T(8,128)(2,1)}, bf16[32,16384]{1,0:T(8,128)(2,1)}, bf16[32,16384]{1,0:T(8,128)(2,1)}, bf16[32,16384]{1,0:T(8,128)(2,1)}), (bf16[32,16384]{1,0:T(8,128)(2,1)}, bf16[32,16384]{1,0:T(8,128)(2,1)}, ...) | async-done | bytes 4194320 | tf_op jit(solution)/shard_map/psum | solution.py:16
  511.1 23.1 %fusion.14 = f32[512,32]{1,0:T(8,128)S(1)} fusion(bf16[32,16384]{1,0:T(8,128)(2,1)} %get-tuple-element.14, bf16[64,8,128,128]{3,2,1,0:T(8,128)(2,1)} %bitcast.404), kind=kOutput, calls=%fused_computation.26 | convolution fusion | flops 536870912 | bytes 17891328 | tf_op jit(solution)/shard_map/dot_general | solution.py:80
  534.2 21.5 %fusion.6 = f32[512,32]{1,0:T(8,128)S(1)} fusion(bf16[32,16384]{1,0:T(8,128)(2,1)} %get-tuple-element.14, bf16[64,8,128,128]{3,2,1,0:T(8,128)(2,1)} %bitcast.410), kind=kOutput, calls=%fused_computation.18 | convolution fusion | flops 536870912 | bytes 17891328 | tf_op jit(solution)/shard_map/dot_general | solution.py:80
  555.8 17.4 %fusion.12 = f32[512,32]{1,0:T(8,128)S(1)} fusion(bf16[32,16384]{1,0:T(8,128)(2,1)S(1)} %copy-done.3, bf16[64,8,128,128]{3,2,1,0:T(8,128)(2,1)S(1)} %bitcast.407), kind=kOutput, calls=%fused_computation.24 | convolution fusion | flops 536870912 | bytes 17891328 | tf_op jit(solution)/shard_map/dot_general | solution.py:80
  573.2 21.0 %fusion.4 = f32[512,32]{1,0:T(8,128)S(1)} fusion(bf16[32,16384]{1,0:T(8,128)(2,1)} %get-tuple-element.13, bf16[64,8,128,128]{3,2,1,0:T(8,128)(2,1)} %bitcast.411), kind=kOutput, calls=%fused_computation.16 | convolution fusion | flops 536870912 | bytes 17891328 | tf_op jit(solution)/shard_map/dot_general | solution.py:80
  594.2 18.6 %fusion.10 = f32[512,32]{1,0:T(8,128)S(1)} fusion(bf16[32,16384]{1,0:T(8,128)(2,1)} %get-tuple-element.12, bf16[64,8,128,128]{3,2,1,0:T(8,128)(2,1)S(1)} %bitcast.408), kind=kOutput, calls=%fused_computation.22 | convolution fusion | flops 536870912 | bytes 17891328 | tf_op jit(solution)/shard_map/dot_general | solution.py:80
  612.8 21.0 %fusion.2 = f32[512,32]{1,0:T(8,128)S(1)} fusion(bf16[32,16384]{1,0:T(8,128)(2,1)} %get-tuple-element.12, bf16[64,8,128,128]{3,2,1,0:T(8,128)(2,1)} %bitcast.412), kind=kOutput, calls=%fused_computation.14 | convolution fusion | flops 536870912 | bytes 17891328 | tf_op jit(solution)/shard_map/dot_general | solution.py:80
  633.8 18.4 %fusion.8 = f32[512,32]{1,0:T(8,128)S(1)} fusion(bf16[32,16384]{1,0:T(8,128)(2,1)} %get-tuple-element.11, bf16[64,8,128,128]{3,2,1,0:T(8,128)(2,1)S(1)} %bitcast.409), kind=kOutput, calls=%fused_computation.20 | convolution fusion | flops 536870912 | bytes 17891328 | tf_op jit(solution)/shard_map/dot_general | solution.py:80
  652.2 20.8 %fusion = f32[512,32]{1,0:T(8,128)S(1)} fusion(bf16[32,16384]{1,0:T(8,128)(2,1)} %get-tuple-element.11, bf16[64,8,128,128]{3,2,1,0:T(8,128)(2,1)} %bitcast.413), kind=kOutput, calls=%fused_computation.12 | convolution fusion | flops 536870912 | bytes 17891328 | tf_op jit(solution)/shard_map/dot_general | solution.py:80
  (138 shorter events, 123.3 us)
Async XLA Ops:
  12.0 22.1 %all-to-all-start.6 = ((bf16[8,6,32]{2,1,0:T(8,128)(2,1)}), bf16[8,6,32]{2,1,0:T(8,128)(2,1)S(1)}, u32[]{:S(2)}, u32[]{:S(2)}) async-start(bf16[8,6,32]{2,1,0:T(8,128)(2,1)} %all_to_all.60), calls=%async_computation.6 | async-start | bytes 32768 | tf_op jit(solution)/shard_map/all_to_all | solution.py:63
  34.1 10.2 %all-to-all-start.4 = ((bf16[8,6,32]{2,1,0:T(8,128)(2,1)}), bf16[8,6,32]{2,1,0:T(8,128)(2,1)S(1)}, u32[]{:S(2)}, u32[]{:S(2)}) async-start(bf16[8,6,32]{2,1,0:T(8,128)(2,1)} %all_to_all.56), calls=%async_computation.4 | async-start | bytes 32768 | tf_op jit(solution)/shard_map/all_to_all | solution.py:63
  44.3 8.3 %all-to-all-start.2 = ((bf16[8,6,32]{2,1,0:T(8,128)(2,1)}), bf16[8,6,32]{2,1,0:T(8,128)(2,1)S(1)}, u32[]{:S(2)}, u32[]{:S(2)}) async-start(bf16[8,6,32]{2,1,0:T(8,128)(2,1)} %all_to_all.52), calls=%async_computation.2 | async-start | bytes 32768 | tf_op jit(solution)/shard_map/all_to_all | solution.py:63
  52.6 8.3 %all-to-all-start = ((bf16[8,6,32]{2,1,0:T(8,128)(2,1)}), bf16[8,6,32]{2,1,0:T(8,128)(2,1)S(1)}, u32[]{:S(2)}, u32[]{:S(2)}) async-start(bf16[8,6,32]{2,1,0:T(8,128)(2,1)} %all_to_all.48), calls=%async_computation | async-start | bytes 32768 | tf_op jit(solution)/shard_map/all_to_all | solution.py:63
  61.0 31.4 %all-to-all-start.7 = ((bf16[8,6,16384]{2,1,0:T(8,128)(2,1)}), bf16[8,6,16384]{2,1,0:T(8,128)(2,1)}, u32[]{:S(2)}, u32[]{:S(2)}) async-start(bf16[8,6,16384]{2,1,0:T(8,128)(2,1)} %all_to_all.62), calls=%async_computation.7 | async-start | bytes 4194304 | tf_op jit(solution)/shard_map/all_to_all | solution.py:62
  92.4 31.4 %all-to-all-start.5 = ((bf16[8,6,16384]{2,1,0:T(8,128)(2,1)}), bf16[8,6,16384]{2,1,0:T(8,128)(2,1)}, u32[]{:S(2)}, u32[]{:S(2)}) async-start(bf16[8,6,16384]{2,1,0:T(8,128)(2,1)} %all_to_all.58), calls=%async_computation.5 | async-start | bytes 4194304 | tf_op jit(solution)/shard_map/all_to_all | solution.py:62
  123.8 31.4 %all-to-all-start.3 = ((bf16[8,6,16384]{2,1,0:T(8,128)(2,1)}), bf16[8,6,16384]{2,1,0:T(8,128)(2,1)}, u32[]{:S(2)}, u32[]{:S(2)}) async-start(bf16[8,6,16384]{2,1,0:T(8,128)(2,1)} %all_to_all.54), calls=%async_computation.3 | async-start | bytes 4194304 | tf_op jit(solution)/shard_map/all_to_all | solution.py:62
  155.2 31.5 %all-to-all-start.1 = ((bf16[8,6,16384]{2,1,0:T(8,128)(2,1)}), bf16[8,6,16384]{2,1,0:T(8,128)(2,1)}, u32[]{:S(2)}, u32[]{:S(2)}) async-start(bf16[8,6,16384]{2,1,0:T(8,128)(2,1)} %all_to_all.50), calls=%async_computation.1 | async-start | bytes 4194304 | tf_op jit(solution)/shard_map/all_to_all | solution.py:62
  159.6 31.0 %copy-start.1 = (s32[4]{0:T(128)S(1)}, s32[4]{0:T(128)}, u32[]{:S(2)}) copy-start(s32[4]{0:T(128)} %param.17) | copy-start | bytes 52
  159.6 237.9 %all-reduce.6.cloned.1.call-start = ((), (), s32[]{:S(2)}) async-start(), calls=%async_computation.8 | async-start | bytes 16777216 | tf_op jit(solution)/shard_map/psum | solution.py:69
  190.6 320.5 %all-reduce.8.cloned.1.call-start = ((), (), s32[]{:S(2)}) async-start(), calls=%async_computation.9 | async-start | bytes 8388608 | tf_op jit(solution)/shard_map/psum | solution.py:16
  194.0 56.7 %copy-start.2 = (f32[32]{0:T(128)S(1)}, f32[32]{0:T(128)}, u32[]{:S(2)}) copy-start(f32[32]{0:T(128)} %param.12) | copy-start | bytes 388
  195.2 202.3 %copy-start = (f32[32,16384]{1,0:T(8,128)S(1)}, f32[32,16384]{1,0:T(8,128)}, u32[]{:S(2)}) copy-start(f32[32,16384]{1,0:T(8,128)} %param.11) | copy-start | bytes 6291460
  511.1 44.7 %slice-start = ((s8[16777216]{0:T(1024)(128)(4,1)}), s8[4194304]{0:T(1024)(128)(4,1)S(1)}, s32[]{:S(2)}) async-start(s8[16777216]{0:T(1024)(128)(4,1)} %bitcast.405), calls=%async_computation.10 | async-start | bytes 8388608
  511.1 44.7 %slice-start.1 = ((s8[16777216]{0:T(1024)(128)(4,1)}), s8[4194304]{0:T(1024)(128)(4,1)S(1)}, s32[]{:S(2)}) async-start(s8[16777216]{0:T(1024)(128)(4,1)} %bitcast.405), calls=%async_computation.11 | async-start | bytes 8388608
  534.2 21.6 %copy-start.3 = (bf16[32,16384]{1,0:T(8,128)(2,1)S(1)}, bf16[32,16384]{1,0:T(8,128)(2,1)}, u32[]{:S(2)}) copy-start(bf16[32,16384]{1,0:T(8,128)(2,1)} %get-tuple-element.13) | copy-start | bytes 3145732
  534.2 21.6 %slice-start.2 = ((s8[16777216]{0:T(1024)(128)(4,1)}), s8[4194304]{0:T(1024)(128)(4,1)S(1)}, s32[]{:S(2)}) async-start(s8[16777216]{0:T(1024)(128)(4,1)} %bitcast.405), calls=%async_computation.12 | async-start | bytes 8388608
  534.2 21.6 %slice-start.3 = ((s8[16777216]{0:T(1024)(128)(4,1)}), s8[4194304]{0:T(1024)(128)(4,1)S(1)}, s32[]{:S(2)}) async-start(s8[16777216]{0:T(1024)(128)(4,1)} %bitcast.405), calls=%async_computation.13 | async-start | bytes 8388608
Sparse Core Ops, SparseCore 0:
  190.7 206.8 all-reduce.5
  406.8 104.1 all-reduce.7
where the time goes:
time: 691 us; the launch traced here: 682 us
  waiting for transfers between devices  266 us (38%)
  matrix products  182 us (26%)
  local copies, waits for them, and re-layouts  133 us (19%)
  starting transfers between devices  35.9 us (5%)
  blocking collectives  34.7 us (5%)
  between operations  17.4 us (3%)
  other arithmetic  13.8 us (2%)
    dot_general x8, matrix products, per_device(): lax.dot_general(rolled, refs, (((1,), (1,)), ((), ())), preferred_element...  162 us
    psum x1, waiting for transfers between devices, per_device(): totals, mass = lax.psum((partial_value, counts), 'dom')  147 us
    all_to_all x4, waiting for transfers between devices, per_device(): lax.all_to_all(send_images, 'cls', split_axis=0, concat_axis=0, tiled=True)  54.9 us
    psum x1, waiting for transfers between devices, from_root(): return lax.psum(block, axis)  53.9 us
    gather x8, local copies, waits for them, and re-layouts, rotate_each(): return jnp.take_along_axis(images, index[:, None, :], axis=2)  45.6 us
    unnamed x49, local copies, waits for them, and re-layouts  43.7 us
    psum x1, blocking collectives, per_device(): totals, mass = lax.psum((partial_value, counts), 'dom')  34.7 us
    another operation x3, local copies, waits for them, and re-layouts, per_device(): rolled = jnp.stack(views, axis=1).reshape(per_dev * count, pixels)  29.9 us
  transfers between devices with their start and end apart: 10, of which 9 were waited for; matrix products, arithmetic and copies ran while one was open for 20% of the time, Pallas kernels for 0%

commit v1 on v0

--- a/solution.py
+++ b/solution.py
@@ -13,7 +13,7 @@
 
 def from_root(block, axis, owner):
     block = jnp.where(lax.axis_index(axis) == owner, block, jnp.zeros_like(block))
-    return lax.psum(block, axis)
+    return lax.all_gather(block, axis).sum(axis=0)
 
 
 def rotate_each(images, shifts, angles):

time: 691 us -> 854 us (1.24)
  waiting for transfers between devices: 266 us -> 411 us
  other arithmetic: 13.8 us -> 33.7 us
  matrix products: 182 us -> 172 us
  local copies, waits for them, and re-layouts: 133 us -> 142 us
    all_gather x0 -> x4, waiting for transfers between devices: none -> 177 us  [from_root(): return lax.all_gather(block, axis).sum(axis=0)]
    psum x1 -> x0, waiting for transfers between devices: 53.9 us -> none  [from_root(): return lax.psum(block, axis)]
    reduce_sum x0 -> x4, other arithmetic: none -> 20.1 us  [from_root(): return lax.all_gather(block, axis).sum(axis=0)]
    psum x1, waiting for transfers between devices: 147 us -> 167 us  [per_device(): totals, mass = lax.psum((partial_value, counts), 'dom')]
    unnamed x49 -> x53, local copies, waits for them, and re-layouts: 43.7 us -> 43.7 us
  transfers between devices with their start and end apart: 10 -> 13, of which waited for: 9 -> 11; matrix products, arithmetic and copies ran while one was open for 20% -> 33% of each run, Pallas kernels for 0% -> 0%
where the time goes in v1:
time: 854 us; the launch traced here: 846 us
  waiting for transfers between devices  411 us (48%)
  matrix products  172 us (20%)
  local copies, waits for them, and re-layouts  142 us (17%)
  blocking collectives  35.9 us (4%)
  starting transfers between devices  35.3 us (4%)
  other arithmetic  33.7 us (4%)
  between operations  17.2 us (2%)
    all_gather x4, waiting for transfers between devices, from_root(): return lax.all_gather(block, axis).sum(axis=0)  177 us
    psum x1, waiting for transfers between devices, per_device(): totals, mass = lax.psum((partial_value, counts), 'dom')  167 us
    dot_general x8, matrix products, per_device(): lax.dot_general(rolled, refs, (((1,), (1,)), ((), ())), preferred_element...  154 us
    all_to_all x4, waiting for transfers between devices, per_device(): lax.all_to_all(send_images, 'cls', split_axis=0, concat_axis=0, tiled=True)  54.7 us
    gather x8, local copies, waits for them, and re-layouts, rotate_each(): return jnp.take_along_axis(images, index[:, None, :], axis=2)  45.6 us
    unnamed x53, local copies, waits for them, and re-layouts  43.7 us
    another operation x3, local copies, waits for them, and re-layouts, per_device(): rolled = jnp.stack(views, axis=1).reshape(per_dev * count, pixels)  38.2 us
    psum x1, blocking collectives, per_device(): totals, mass = lax.psum((partial_value, counts), 'dom')  35.9 us
  transfers between devices with their start and end apart: 13, of which 11 were waited for; matrix products, arithmetic and copies ran while one was open for 33% of the time, Pallas kernels for 0%

profile of v1, /device:TPU:1, one launch (start us, length us, event | category | flops | bytes accessed | tf_op | source)
XLA Modules:
  0.0 845.9 jit_solution(4089737253499171359)
XLA Ops:
  12.0 6.4 all-to-all-start.6
  20.8 11.1 %gather_fusion.3 = bf16[2048,128]{1,0:T(8,128)(2,1)S(1)} fusion(bf16[16,128,128]{1,2,0:T(8,128)(2,1)S(1)} %copy.50, s32[2048]{0:T(1024)S(1)} %get-tuple-element.111), kind=kCustom, calls=%fused_computation.3.clone | custom fusion | bytes 1064960 | tf_op jit(solution)/shard_map/jit(take_along_axis)/gather | solution.py:22
  64.6 11.1 %gather_fusion.2 = bf16[2048,128]{1,0:T(8,128)(2,1)S(1)} fusion(bf16[16,128,128]{1,2,0:T(8,128)(2,1)S(1)} %copy.50, s32[2048]{0:T(1024)S(1)} %get-tuple-element.112), kind=kCustom, calls=%fused_computation.2.clone | custom fusion | bytes 1064960 | tf_op jit(solution)/shard_map/jit(take_along_axis)/gather | solution.py:22
  78.3 13.3 %all-to-all-done.7 = bf16[8,6,16384]{2,1,0:T(8,128)(2,1)} async-done(((bf16[8,6,16384]{2,1,0:T(8,128)(2,1)}), bf16[8,6,16384]{2,1,0:T(8,128)(2,1)}, u32[]{:S(2)}, u32[]{:S(2)}) %all-to-all-start.7) | async-done | bytes 1572896 | tf_op jit(solution)/shard_map/all_to_all | solution.py:62
  96.1 11.1 %gather_fusion.1 = bf16[2048,128]{1,0:T(8,128)(2,1)S(1)} fusion(bf16[16,128,128]{1,2,0:T(8,128)(2,1)S(1)} %copy.50, s32[2048]{0:T(1024)S(1)} %get-tuple-element.113), kind=kCustom, calls=%fused_computation.1.clone | custom fusion | bytes 1064960 | tf_op jit(solution)/shard_map/jit(take_along_axis)/gather | solution.py:22
  109.8 13.2 %all-to-all-done.5 = bf16[8,6,16384]{2,1,0:T(8,128)(2,1)} async-done(((bf16[8,6,16384]{2,1,0:T(8,128)(2,1)}), bf16[8,6,16384]{2,1,0:T(8,128)(2,1)}, u32[]{:S(2)}, u32[]{:S(2)}) %all-to-all-start.5) | async-done | bytes 1572896 | tf_op jit(solution)/shard_map/all_to_all | solution.py:62
  127.4 11.1 %gather_fusion = bf16[2048,128]{1,0:T(8,128)(2,1)S(1)} fusion(bf16[16,128,128]{1,2,0:T(8,128)(2,1)S(1)} %copy.50, s32[2048]{0:T(1024)S(1)} %get-tuple-element.114), kind=kCustom, calls=%fused_computation.clone | custom fusion | bytes 1064960 | tf_op jit(solution)/shard_map/jit(take_along_axis)/gather | solution.py:22
  141.2 13.3 %all-to-all-done.3 = bf16[8,6,16384]{2,1,0:T(8,128)(2,1)} async-done(((bf16[8,6,16384]{2,1,0:T(8,128)(2,1)}), bf16[8,6,16384]{2,1,0:T(8,128)(2,1)}, u32[]{:S(2)}, u32[]{:S(2)}) %all-to-all-start.3) | async-done | bytes 1572896 | tf_op jit(solution)/shard_map/all_to_all | solution.py:62
  170.1 14.9 %all-to-all-done.1 = bf16[8,6,16384]{2,1,0:T(8,128)(2,1)S(1)} async-done(((bf16[8,6,16384]{2,1,0:T(8,128)(2,1)}), bf16[8,6,16384]{2,1,0:T(8,128)(2,1)S(1)}, u32[]{:S(2)}, u32[]{:S(2)}) %all-to-all-start.1) | async-done | bytes 1572896 | tf_op jit(solution)/shard_map/all_to_all | solution.py:62
  189.4 35.9 %all-reduce = (f32[32]{0:T(128)S(1)}, f32[32]{0:T(128)S(1)}, f32[32]{0:T(128)S(1)}, f32[32]{0:T(128)S(1)}) all-reduce(f32[32]{0:T(128)S(1)} %convert_reduce_fusion, f32[32]{0:T(128)S(1)} %convert_reduce_fusion.1, f32[32]{0:T(128)S(1)} %convert_reduce_fusion.2, f32[32]{0:T(128)S(1)} %convert_reduce_fusion.3), channel_id=1, replica_groups=mesh['dom'=16,'cls'=8] {'dom'}, use_global_device_ids=true, to_apply=%region_22.24 | all-reduce | flops 128 | bytes 1024 | tf_op jit(solution)/shard_map/psum | solution.py:69
  225.3 166.9 %all-reduce.4.cloned.1.call-done = (f32[32,16384]{1,0:T(8,128)}, f32[32,16384]{1,0:T(8,128)}, f32[32,16384]{1,0:T(8,128)}, f32[32,16384]{1,0:T(8,128)}) async-done(((f32[32,16384]{1,0:T(8,128)}, f32[32,16384]{1,0:T(8,128)}, f32[32,16384]{1,0:T(8,128)}, f32[32,16384]{1,0:T(8,128)}), (f32[32,16384]{1,0:T(8,128)}, f32[32,16384]{1,0:T(8,128)}, f32[32,16384]{1,0:T(8,128)}, ...) | async-done | bytes 8388624 | tf_op jit(solution)/shard_map/psum | solution.py:69
  448.3 22.5 %copy.48 = bf16[16,32,128,128]{3,2,1,0:T(8,128)(2,1)} copy(bf16[16,32,128,128]{3,2,0,1:T(8,128)(2,1)} %get-tuple-element.17) | data formatting | bytes 33554432 | tf_op jit(solution)/shard_map/stack | solution.py:79
  470.9 14.2 %copy.55 = bf16[16,32,128,128]{3,2,1,0:T(8,128)(2,1)} copy(bf16[16,32,128,128]{3,2,0,1:T(8,128)(2,1)} %get-tuple-element.18) | data formatting | bytes 33554432 | tf_op jit(solution)/shard_map/stack | solution.py:79
  491.8 87.7 %all-gather.11.cloned.1.call-done = bf16[256,16384]{1,0:T(8,128)(2,1)} async-done(((bf16[32,16384]{1,0:T(8,128)(2,1)}), bf16[256,16384]{1,0:T(8,128)(2,1)}) %all-gather.11.cloned.1.call-update) | async-done | bytes 8388624 | tf_op jit(solution)/shard_map/all_gather | solution.py:16
  584.2 87.5 %all-gather.13.cloned.1.call-done = bf16[256,16384]{1,0:T(8,128)(2,1)} async-done(((bf16[32,16384]{1,0:T(8,128)(2,1)}), bf16[256,16384]{1,0:T(8,128)(2,1)}) %all-gather.13.cloned.1.call-update) | async-done | bytes 8388624 | tf_op jit(solution)/shard_map/all_gather | solution.py:16
  671.7 5.9 reduce_sum.128
  677.7 17.6 %fusion.14 = f32[512,32]{1,0:T(8,128)} fusion(bf16[32,16384]{1,0:T(8,128)(2,1)S(1)} %reduce_sum.122, bf16[64,8,128,128]{3,2,1,0:T(8,128)(2,1)} %bitcast.408), kind=kOutput, calls=%fused_computation.26 | convolution fusion | flops 536870912 | bytes 17891328 | tf_op jit(solution)/shard_map/dot_general | solution.py:80
  695.2 18.2 %fusion.6 = f32[512,32]{1,0:T(8,128)} fusion(bf16[32,16384]{1,0:T(8,128)(2,1)S(1)} %reduce_sum.122, bf16[64,8,128,128]{3,2,1,0:T(8,128)(2,1)} %bitcast.414), kind=kOutput, calls=%fused_computation.18 | convolution fusion | flops 536870912 | bytes 17891328 | tf_op jit(solution)/shard_map/dot_general | solution.py:80
  713.5 17.8 %fusion.12 = f32[512,32]{1,0:T(8,128)} fusion(bf16[32,16384]{1,0:T(8,128)(2,1)S(1)} %reduce_sum.125, bf16[64,8,128,128]{3,2,1,0:T(8,128)(2,1)S(1)} %bitcast.412), kind=kOutput, calls=%fused_computation.24 | convolution fusion | flops 536870912 | bytes 17891328 | tf_op jit(solution)/shard_map/dot_general | solution.py:80
  731.3 21.2 %fusion.4 = f32[512,32]{1,0:T(8,128)S(1)} fusion(bf16[32,16384]{1,0:T(8,128)(2,1)S(1)} %reduce_sum.125, bf16[64,8,128,128]{3,2,1,0:T(8,128)(2,1)} %bitcast.415), kind=kOutput, calls=%fused_computation.16 | convolution fusion | flops 536870912 | bytes 17891328 | tf_op jit(solution)/shard_map/dot_general | solution.py:80
  752.6 17.1 %fusion.10 = f32[512,32]{1,0:T(8,128)S(1)} fusion(bf16[32,16384]{1,0:T(8,128)(2,1)S(1)} %copy-done, bf16[64,8,128,128]{3,2,1,0:T(8,128)(2,1)S(1)} %bitcast.413), kind=kOutput, calls=%fused_computation.22 | convolution fusion | flops 536870912 | bytes 17891328 | tf_op jit(solution)/shard_map/dot_general | solution.py:80
  769.7 20.7 %fusion.2 = f32[512,32]{1,0:T(8,128)S(1)} fusion(bf16[32,16384]{1,0:T(8,128)(2,1)S(1)} %copy-done, bf16[64,8,128,128]{3,2,1,0:T(8,128)(2,1)} %bitcast.416), kind=kOutput, calls=%fused_computation.14 | convolution fusion | flops 536870912 | bytes 17891328 | tf_op jit(solution)/shard_map/dot_general | solution.py:80
  795.1 20.8 %fusion.8 = f32[512,32]{1,0:T(8,128)S(1)} fusion(bf16[32,16384]{1,0:T(8,128)(2,1)S(1)} %reduce_sum.131, bf16[64,8,128,128]{3,2,1,0:T(8,128)(2,1)} %bitcast.409), kind=kOutput, calls=%fused_computation.20 | convolution fusion | flops 536870912 | bytes 17891328 | tf_op jit(solution)/shard_map/dot_general | solution.py:80
  816.0 20.9 %fusion = f32[512,32]{1,0:T(8,128)S(1)} fusion(bf16[32,16384]{1,0:T(8,128)(2,1)S(1)} %reduce_sum.131, bf16[64,8,128,128]{3,2,1,0:T(8,128)(2,1)} %bitcast.417), kind=kOutput, calls=%fused_computation.12 | convolution fusion | flops 536870912 | bytes 17891328 | tf_op jit(solution)/shard_map/dot_general | solution.py:80
  (155 shorter events, 148.1 us)
Async XLA Ops:
  12.0 21.3 %all-to-all-start.6 = ((bf16[8,6,32]{2,1,0:T(8,128)(2,1)}), bf16[8,6,32]{2,1,0:T(8,128)(2,1)S(1)}, u32[]{:S(2)}, u32[]{:S(2)}) async-start(bf16[8,6,32]{2,1,0:T(8,128)(2,1)} %all_to_all.60), calls=%async_computation.6 | async-start | bytes 32768 | tf_op jit(solution)/shard_map/all_to_all | solution.py:63
  33.3 10.2 %all-to-all-start.4 = ((bf16[8,6,32]{2,1,0:T(8,128)(2,1)}), bf16[8,6,32]{2,1,0:T(8,128)(2,1)S(1)}, u32[]{:S(2)}, u32[]{:S(2)}) async-start(bf16[8,6,32]{2,1,0:T(8,128)(2,1)} %all_to_all.56), calls=%async_computation.4 | async-start | bytes 32768 | tf_op jit(solution)/shard_map/all_to_all | solution.py:63
  43.5 8.3 all-to-all-start.2
  51.9 8.3 all-to-all-start
  60.2 31.4 %all-to-all-start.7 = ((bf16[8,6,16384]{2,1,0:T(8,128)(2,1)}), bf16[8,6,16384]{2,1,0:T(8,128)(2,1)}, u32[]{:S(2)}, u32[]{:S(2)}) async-start(bf16[8,6,16384]{2,1,0:T(8,128)(2,1)} %all_to_all.62), calls=%async_computation.7 | async-start | bytes 4194304 | tf_op jit(solution)/shard_map/all_to_all | solution.py:62
  91.6 31.4 %all-to-all-start.5 = ((bf16[8,6,16384]{2,1,0:T(8,128)(2,1)}), bf16[8,6,16384]{2,1,0:T(8,128)(2,1)}, u32[]{:S(2)}, u32[]{:S(2)}) async-start(bf16[8,6,16384]{2,1,0:T(8,128)(2,1)} %all_to_all.58), calls=%async_computation.5 | async-start | bytes 4194304 | tf_op jit(solution)/shard_map/all_to_all | solution.py:62
  123.0 31.4 %all-to-all-start.3 = ((bf16[8,6,16384]{2,1,0:T(8,128)(2,1)}), bf16[8,6,16384]{2,1,0:T(8,128)(2,1)}, u32[]{:S(2)}, u32[]{:S(2)}) async-start(bf16[8,6,16384]{2,1,0:T(8,128)(2,1)} %all_to_all.54), calls=%async_computation.3 | async-start | bytes 4194304 | tf_op jit(solution)/shard_map/all_to_all | solution.py:62
  154.4 30.6 %all-to-all-start.1 = ((bf16[8,6,16384]{2,1,0:T(8,128)(2,1)}), bf16[8,6,16384]{2,1,0:T(8,128)(2,1)S(1)}, u32[]{:S(2)}, u32[]{:S(2)}) async-start(bf16[8,6,16384]{2,1,0:T(8,128)(2,1)} %all_to_all.50), calls=%async_computation.1 | async-start | bytes 4194304 | tf_op jit(solution)/shard_map/all_to_all | solution.py:62
  158.1 29.3 %copy-start.4 = (s32[4]{0:T(128)S(1)}, s32[4]{0:T(128)}, u32[]{:S(2)}) copy-start(s32[4]{0:T(128)} %param.17) | copy-start | bytes 52
  158.1 67.3 %copy-start.5 = (f32[32]{0:T(128)S(1)}, f32[32]{0:T(128)}, u32[]{:S(2)}) copy-start(f32[32]{0:T(128)} %param.12) | copy-start | bytes 388
  158.1 234.2 %all-reduce.4.cloned.1.call-start = ((), (), s32[]{:S(2)}) async-start(), calls=%async_computation.12 | async-start | bytes 16777216 | tf_op jit(solution)/shard_map/psum | solution.py:69
  187.3 299.8 %all-gather.9.cloned.1.call-start = ((), (), s32[]{:S(2)}) async-start(), calls=%async_computation.8 | async-start | bytes 9437184 | tf_op jit(solution)/shard_map/all_gather | solution.py:16
  397.2 182.3 %all-gather.11.cloned.1.call-start = ((), (), s32[]{:S(2)}) async-start(), calls=%async_computation.9 | async-start | bytes 9437184 | tf_op jit(solution)/shard_map/all_gather | solution.py:16
  397.9 273.8 %all-gather.13.cloned.1.call-start = ((), (), s32[]{:S(2)}) async-start(), calls=%async_computation.10 | async-start | bytes 9437184 | tf_op jit(solution)/shard_map/all_gather | solution.py:16
  404.1 386.3 %all-gather.15.cloned.1.call-start = ((), (), s32[]{:S(2)}) async-start(), calls=%async_computation.11 | async-start | bytes 9437184 | tf_op jit(solution)/shard_map/all_gather | solution.py:16
  677.7 35.8 %slice-start = ((s8[16777216]{0:T(1024)(128)(4,1)}), s8[4194304]{0:T(1024)(128)(4,1)S(1)}, s32[]{:S(2)}) async-start(s8[16777216]{0:T(1024)(128)(4,1)} %bitcast.410), calls=%async_computation.13 | async-start | bytes 8388608
  677.7 35.8 %slice-start.1 = ((s8[16777216]{0:T(1024)(128)(4,1)}), s8[4194304]{0:T(1024)(128)(4,1)S(1)}, s32[]{:S(2)}) async-start(s8[16777216]{0:T(1024)(128)(4,1)} %bitcast.410), calls=%async_computation.14 | async-start | bytes 8388608
  695.2 18.2 %slice-start.2 = ((s8[16777216]{0:T(1024)(128)(4,1)}), s8[4194304]{0:T(1024)(128)(4,1)S(1)}, s32[]{:S(2)}) async-start(s8[16777216]{0:T(1024)(128)(4,1)} %bitcast.410), calls=%async_computation.15 | async-start | bytes 8388608
  695.2 18.2 %slice-start.3 = ((s8[16777216]{0:T(1024)(128)(4,1)}), s8[4194304]{0:T(1024)(128)(4,1)S(1)}, s32[]{:S(2)}) async-start(s8[16777216]{0:T(1024)(128)(4,1)} %bitcast.410), calls=%async_computation.16 | async-start | bytes 8388608
  731.3 21.3 %copy-start = (bf16[32,16384]{1,0:T(8,128)(2,1)S(1)}, bf16[32,16384]{1,0:T(8,128)(2,1)}, u32[]{:S(2)}) copy-start(bf16[32,16384]{1,0:T(8,128)(2,1)} %reduce_sum.128) | copy-start | bytes 3145732
  815.9 20.9 %copy-start.3 = (f32[512,32]{1,0:T(8,128)S(1)}, f32[512,32]{1,0:T(8,128)}, u32[]{:S(2)}) copy-start(f32[512,32]{1,0:T(8,128)} %fusion.14) | copy-start | bytes 196612
  815.9 21.0 %copy-start.1 = (f32[512,32]{1,0:T(8,128)S(1)}, f32[512,32]{1,0:T(8,128)}, u32[]{:S(2)}) copy-start(f32[512,32]{1,0:T(8,128)} %fusion.6) | copy-start | bytes 196612
  816.0 21.2 %copy-start.2 = (f32[512,32]{1,0:T(8,128)S(1)}, f32[512,32]{1,0:T(8,128)}, u32[]{:S(2)}) copy-start(f32[512,32]{1,0:T(8,128)} %fusion.12) | copy-start | bytes 196612
Sparse Core Ops, SparseCore 0:
  187.4 204.7 all-reduce.3
  397.3 89.7 all-gather.8
  488.8 90.6 all-gather.10
  581.0 90.6 all-gather.12
  673.2 90.6 all-gather.14
